TPU v7x, 512 devices: a whole 4x8x8 slice. The times are simulated.
512 devices in a mesh: seq: 64 (over z_hi, y, core), tp: 8 (over x, z_lo).
Axes of the slice: x: 4, y: 8, z: 8 (z_hi: 4, z_lo: 2; z = z_hi * 2 + z_lo), core: 2. Of those that a mesh axis runs over, the one named last changes fastest.
Arguments:
- query_proj: bfloat16 [16384, 3072], P('seq', 'tp'), may hold values from -8 to 8
- key_proj: bfloat16 [16384, 3072], P('seq', 'tp'), may hold values from -8 to 8
- value_proj: bfloat16 [16384, 3072], P('seq', 'tp'), may hold values from -6 to 6
- hidden: bfloat16 [16384, 3072], P('seq', 'tp'), may hold values from -2 to 2
- out_weight: bfloat16 [3072, 3072], P('tp'), may hold values from -0.109375 to 0.109375
- norm_gain: bfloat16 [3072], P('tp'), may hold values from 0.099609375 to 1.8984375
- segment_ids: int32 [16384], P('seq'), may hold values from 0 to 31, never falling along the last dimension, each value on 1 to 8192 neighbouring positions
- pad_mask: int32 [16384], P('seq'), may hold values 0 or 1
- page_table: int32 [128], P('seq'), may hold values from 0 to 1, as said below
Outputs:
- hidden_out: bfloat16 [16384, 3072], P('seq', 'tp')
- normed: bfloat16 [16384, 3072], P('seq', 'tp')
- kv_pages: bfloat16 [128, 2, 128, 3072], P('seq', None, None, 'tp')
Inputs may be any that keep to these rules, and one draw needn't show every extreme that they name: `segment_ids`: never falling along the tokens; each of the 32 prompts has 1 to 8192 tokens, one exactly 8192. `page_table`: the 2 pages of each aligned block of 2 pages name each slot once.
All inputs are finite; a program needn't handle non-finite values. No bound on the sum of `pad_mask` on one device may be relied on, other than what follows from the above.
Results may differ from a plain program's by a relative error of at most 0.014.
Values may be sent and summed in bfloat16 or wider, within the bound.
No kernel may reach another device: no remote copies, remote signals or barrier semaphores. Data moves between devices by JAX's collectives and lax.ppermute only.
A program may use at most 128 MiB of HBM per device.

v0:
```python
import math
import jax
import jax.numpy as jnp
from jax import lax
from jax.sharding import PartitionSpec as P

D = 3072
HEAD_DIM = 96
PAGE = 128
far_index = 1073741824
masked_score = -1e30
norm_epsilon = 1e-05


def passed_along(block, axis, distance):
    devices = range(lax.axis_size(axis))
    route = [(i - distance, i) for i in devices if i - distance in devices]
    return lax.ppermute(block, axis, route)


def rotate(values_in, position, head_count, head_dim):
    count_rows = values_in.shape[0]
    half_dim = head_dim // 2
    frequency = jnp.exp(
        jnp.arange(half_dim, dtype=jnp.float32) * (-2.0 * math.log(10000.0) / head_dim)
    )
    angles = position.astype(jnp.float32)[:, None] * frequency[None, :]
    cosine = jnp.cos(angles)[:, None, :]
    sine_part = jnp.sin(angles)[:, None, :]
    as_float = values_in.astype(jnp.float32).reshape(count_rows, head_count, head_dim)
    lower_half = as_float[..., :half_dim]
    upper_half = as_float[..., half_dim:]
    rotated = jnp.concatenate(
        [
            lower_half * cosine - upper_half * sine_part,
            upper_half * cosine + lower_half * sine_part,
        ],
        axis=-1,
    )
    return rotated.reshape(count_rows, head_count * head_dim).astype(jnp.bfloat16)


def attend(softmax_state, query_heads, block, visible):
    row_peak, row_total, weighted = softmax_state
    key_count = block.shape[1]
    head_count = query_heads.shape[1]
    key_heads = block[0].reshape(key_count, head_count, HEAD_DIM)
    val_heads = block[1].reshape(key_count, head_count, HEAD_DIM)
    factor = 1.0 / math.sqrt(HEAD_DIM)
    logits = (
        jnp.einsum("qhd,khd->hqk", query_heads, key_heads, preferred_element_type=jnp.float32)
        * factor
    )
    logits = jnp.where(visible[None], logits, masked_score)
    new_peak = jnp.maximum(row_peak, jnp.max(logits, axis=-1))
    rescale = jnp.exp(row_peak - new_peak)
    unnormed = jnp.where(visible[None], jnp.exp(logits - new_peak[..., None]), 0.0)
    row_total = row_total * rescale + jnp.sum(unnormed, axis=-1)
    weighted = weighted * rescale[..., None] + jnp.einsum(
        "hqk,khd->hqd", unnormed.astype(jnp.bfloat16), val_heads, preferred_element_type=jnp.float32
    )
    return (new_peak, row_total, weighted)


def per_device(
    query_proj,
    key_proj,
    value_proj,
    hidden,
    out_weight,
    norm_gain,
    segment_ids,
    pad_mask,
    page_table,
):
    tok_count = query_proj.shape[0]
    feat_count = query_proj.shape[1]
    head_count = feat_count // HEAD_DIM
    seg_count = lax.axis_size("seq") // 2
    reach_count = lax.axis_size("seq") // 2
    device_row = lax.axis_index("seq")
    tok_index = device_row * tok_count + jnp.arange(tok_count, dtype=jnp.int32)
    member = segment_ids[:, None] == jnp.arange(seg_count, dtype=jnp.int32)[None, :]
    local_first = jnp.min(jnp.where(member, tok_index[:, None], far_index), axis=0)
    first_tok = lax.pmin(local_first, "seq")
    position = tok_index - jnp.sum(jnp.where(member, first_tok[None, :], 0), axis=1)
    q_rot = rotate(query_proj, position, head_count, HEAD_DIM)
    k_rot = rotate(key_proj, position, head_count, HEAD_DIM)
    query_heads = q_rot.reshape(tok_count, head_count, HEAD_DIM)
    query_tag = segment_ids + 1
    key_tag = jnp.where(pad_mask == 1, segment_ids + 1, 0)
    tag_rows = -(-tok_count // feat_count)
    tag_block = jnp.pad(key_tag.astype(jnp.bfloat16), (0, tag_rows * feat_count - tok_count))
    own_block = jnp.concatenate(
        [k_rot, value_proj, tag_block.reshape(tag_rows, feat_count)], axis=0
    )
    offsets = jnp.arange(tok_count, dtype=jnp.int32)
    own_visible = (key_tag[None, :] == query_tag[:, None]) & (
        offsets[None, :] <= offsets[:, None]
    ) | (offsets[None, :] == offsets[:, None])
    softmax_state = (
        jnp.full((head_count, tok_count), masked_score, jnp.float32),
        jnp.zeros((head_count, tok_count), jnp.float32),
        jnp.zeros((head_count, tok_count, HEAD_DIM), jnp.float32),
    )
    softmax_state = attend(softmax_state, query_heads, jnp.stack([k_rot, value_proj]), own_visible)
    query_tag_wide = query_tag.astype(jnp.bfloat16)

    def visit_block(current, moved):
        pair = moved[: 2 * tok_count].reshape(2, tok_count, feat_count)
        moved_tags = moved[2 * tok_count :].reshape(-1)[:tok_count]
        visible = moved_tags[None, :] == query_tag_wide[:, None]
        return attend(current, query_heads, pair, visible)

    def cycle_turn(turn_index, loop_state):
        current, moved = loop_state
        following = passed_along(moved, "seq", 1)
        return (visit_block(current, moved), following)

    moved = passed_along(own_block, "seq", 1)
    softmax_state, moved = lax.fori_loop(0, reach_count - 1, cycle_turn, (softmax_state, moved))
    softmax_state = visit_block(softmax_state, moved)
    row_peak, row_total, weighted = softmax_state
    attn = (
        jnp.transpose(weighted / row_total[..., None], (1, 0, 2))
        .reshape(tok_count, feat_count)
        .astype(jnp.bfloat16)
    )
    partial_value = jnp.dot(attn, out_weight, preferred_element_type=jnp.float32)
    feature_width = hidden.shape[1]
    own_sum = lax.psum_scatter(
        partial_value.astype(jnp.bfloat16), "tp", scatter_dimension=1, tiled=True
    ).astype(jnp.float32)
    hidden_out = (hidden.astype(jnp.float32) + own_sum).astype(jnp.bfloat16)
    stream_wide = hidden_out.astype(jnp.float32)
    square_total = lax.psum(jnp.sum(stream_wide * stream_wide, axis=1), "tp")
    normed = (
        stream_wide
        * lax.rsqrt(square_total / D + norm_epsilon)[:, None]
        * norm_gain.astype(jnp.float32)[None, :]
    ).astype(jnp.bfloat16)
    pad_scale = pad_mask.astype(jnp.bfloat16)[:, None]
    page_count = tok_count // PAGE
    stacked = jnp.stack([k_rot * pad_scale, value_proj * pad_scale])
    stacked = stacked.reshape(2, page_count, PAGE, feat_count).transpose(1, 0, 2, 3)
    kv_pages = jnp.zeros_like(stacked).at[page_table].set(stacked)
    return (hidden_out, normed, kv_pages)


def solution(mesh):
    placed = (
        P("seq", "tp"),
        P("seq", "tp"),
        P("seq", "tp"),
        P("seq", "tp"),
        P("tp", None),
        P("tp"),
        P("seq"),
        P("seq"),
        P("seq"),
    )
    return jax.shard_map(
        per_device,
        mesh=mesh,
        in_specs=placed,
        out_specs=(P("seq", "tp"), P("seq", "tp"), P("seq", None, None, "tp")),
        check_vma=False,
    )
```

profile of v0, /device:TPU:8, one launch (start us, length us, event | category | flops | bytes accessed | tf_op | source)
XLA Modules:
  0.0 678.9 jit_solution(2169950836960678962)
XLA Ops:
  8.2 28.3 %pmin.7 = s32[32]{0:T(128)S(1)} all-reduce(s32[32]{0:T(128)S(1)} %select_reduce_fusion.1), channel_id=1, replica_groups=mesh['seq'=64,'tp'=8] {'seq'}, use_global_device_ids=true, to_apply=%region_1.2 | all-reduce | flops 32 | bytes 256 | tf_op jit(solution)/shard_map/pmin | solution.py:85
  50.9 443.5 %while.16 = (s32[]{:T(128)}, f32[4,256]{1,0:T(4,128)S(1)}, f32[4,256]{1,0:T(4,128)S(1)}, f32[4,256,96]{1,2,0:T(8,128)}, bf16[513,384]{1,0:T(8,128)(2,1)}, /*inde...) while((s32[]{:T(128)}, f32[4,256]{1,0:T(4,128)S(1)}, f32[4,256]{1,0:T(4,128)S(1)}, ...), condition=%wide.region_8.9_spmd, body=%wide.region_5.8_spmd.sunk | while | flops 103286784 | bytes 8788605 | solution.py:121
  111.1 3.4 collective-permute-start
  160.9 3.3 collective-permute-start
  210.7 3.5 collective-permute-start
  223.4 9.2 %collective-permute-start = (bf16[513,384]{1,0:T(8,128)(2,1)}, bf16[513,384]{1,0:T(8,128)(2,1)}, u32[]{:S(2)}, u32[]{:S(2)}) collective-permute-start(bf16[513,384]{1,0:T(8,128)(2,1)} %copy.78), channel_id=1, source_target_pairs={{0,8},{8,16},{16,24},{24,32},{32,40},{40,48},{48,56},{56,64},{64,7... | collective-permute-start | bytes 1181960 | tf_op jit(solution)/shard_map/while/body/eval_jaxpr/ppermute | solution.py:18
  241.7 8.9 %collective-permute-start = (bf16[513,384]{1,0:T(8,128)(2,1)}, bf16[513,384]{1,0:T(8,128)(2,1)}, u32[]{:S(2)}, u32[]{:S(2)}) collective-permute-start(bf16[513,384]{1,0:T(8,128)(2,1)} %copy.78), channel_id=1, source_target_pairs={{0,8},{8,16},{16,24},{24,32},{32,40},{40,48},{48,56},{56,64},{64,7... | collective-permute-start | bytes 1181960 | tf_op jit(solution)/shard_map/while/body/eval_jaxpr/ppermute | solution.py:18
  259.8 9.4 %collective-permute-start = (bf16[513,384]{1,0:T(8,128)(2,1)}, bf16[513,384]{1,0:T(8,128)(2,1)}, u32[]{:S(2)}, u32[]{:S(2)}) collective-permute-start(bf16[513,384]{1,0:T(8,128)(2,1)} %copy.78), channel_id=1, source_target_pairs={{0,8},{8,16},{16,24},{24,32},{32,40},{40,48},{48,56},{56,64},{64,7... | collective-permute-start | bytes 1181960 | tf_op jit(solution)/shard_map/while/body/eval_jaxpr/ppermute | solution.py:18
  278.3 9.2 %collective-permute-start = (bf16[513,384]{1,0:T(8,128)(2,1)}, bf16[513,384]{1,0:T(8,128)(2,1)}, u32[]{:S(2)}, u32[]{:S(2)}) collective-permute-start(bf16[513,384]{1,0:T(8,128)(2,1)} %copy.78), channel_id=1, source_target_pairs={{0,8},{8,16},{16,24},{24,32},{32,40},{40,48},{48,56},{56,64},{64,7... | collective-permute-start | bytes 1181960 | tf_op jit(solution)/shard_map/while/body/eval_jaxpr/ppermute | solution.py:18
  296.6 8.4 %collective-permute-start = (bf16[513,384]{1,0:T(8,128)(2,1)}, bf16[513,384]{1,0:T(8,128)(2,1)}, u32[]{:S(2)}, u32[]{:S(2)}) collective-permute-start(bf16[513,384]{1,0:T(8,128)(2,1)} %copy.78), channel_id=1, source_target_pairs={{0,8},{8,16},{16,24},{24,32},{32,40},{40,48},{48,56},{56,64},{64,7... | collective-permute-start | bytes 1181960 | tf_op jit(solution)/shard_map/while/body/eval_jaxpr/ppermute | solution.py:18
  314.2 7.1 %collective-permute-start = (bf16[513,384]{1,0:T(8,128)(2,1)}, bf16[513,384]{1,0:T(8,128)(2,1)}, u32[]{:S(2)}, u32[]{:S(2)}) collective-permute-start(bf16[513,384]{1,0:T(8,128)(2,1)} %copy.78), channel_id=1, source_target_pairs={{0,8},{8,16},{16,24},{24,32},{32,40},{40,48},{48,56},{56,64},{64,7... | collective-permute-start | bytes 1181960 | tf_op jit(solution)/shard_map/while/body/eval_jaxpr/ppermute | solution.py:18
  330.4 5.1 collective-permute-start
  344.7 5.1 collective-permute-start
  358.9 5.1 collective-permute-start
  373.2 5.7 collective-permute-start
  388.1 6.5 collective-permute-start
  403.6 6.5 collective-permute-start
  419.3 6.4 collective-permute-start
  434.7 6.3 collective-permute-start
  450.2 6.2 collective-permute-start
  465.5 6.2 collective-permute-start
  480.8 6.2 collective-permute-start
  504.7 146.8 %reduce-scatter.4.cloned.1.call-done = bf16[384,256]{1,0:T(8,128)(2,1)} async-done(((bf16[3072,256]{1,0:T(8,128)(2,1)}), bf16[384,256]{1,0:T(8,128)(2,1)}) %reduce-scatter.4.cloned.1.call-update) | async-done | bytes 196624
  652.8 18.4 %psum.7 = f32[256]{0:T(256)S(1)} all-reduce(f32[256]{0:T(256)S(1)} %get-tuple-element.63), channel_id=1, replica_groups=mesh['seq'=64,'tp'=8] {'tp'}, use_global_device_ids=true, to_apply=%region_13.14 | all-reduce | flops 256 | bytes 2048 | tf_op jit(solution)/shard_map/psum | solution.py:136
  (497 shorter events, 341.9 us)
Async XLA Ops:
  7.2 644.4 %reduce-scatter.4.cloned.1.call-start = ((), (), s32[]{:S(2)}) async-start(), calls=%async_computation.1 | async-start | bytes 1769472
  111.1 10.7 %collective-permute-start = (bf16[513,384]{1,0:T(8,128)(2,1)}, bf16[513,384]{1,0:T(8,128)(2,1)}, u32[]{:S(2)}, u32[]{:S(2)}) collective-permute-start(bf16[513,384]{1,0:T(8,128)(2,1)} %copy.78), channel_id=1, source_target_pairs={{0,8},{8,16},{16,24},{24,32},{32,40},{40,48},{48,56},{56,64},{64,7... | collective-permute-start | bytes 1181960 | tf_op jit(solution)/shard_map/while/body/eval_jaxpr/ppermute | solution.py:18
  123.6 10.7 %collective-permute-start = (bf16[513,384]{1,0:T(8,128)(2,1)}, bf16[513,384]{1,0:T(8,128)(2,1)}, u32[]{:S(2)}, u32[]{:S(2)}) collective-permute-start(bf16[513,384]{1,0:T(8,128)(2,1)} %copy.78), channel_id=1, source_target_pairs={{0,8},{8,16},{16,24},{24,32},{32,40},{40,48},{48,56},{56,64},{64,7... | collective-permute-start | bytes 1181960 | tf_op jit(solution)/shard_map/while/body/eval_jaxpr/ppermute | solution.py:18
  160.9 10.7 %collective-permute-start = (bf16[513,384]{1,0:T(8,128)(2,1)}, bf16[513,384]{1,0:T(8,128)(2,1)}, u32[]{:S(2)}, u32[]{:S(2)}) collective-permute-start(bf16[513,384]{1,0:T(8,128)(2,1)} %copy.78), channel_id=1, source_target_pairs={{0,8},{8,16},{16,24},{24,32},{32,40},{40,48},{48,56},{56,64},{64,7... | collective-permute-start | bytes 1181960 | tf_op jit(solution)/shard_map/while/body/eval_jaxpr/ppermute | solution.py:18
  173.4 10.7 %collective-permute-start = (bf16[513,384]{1,0:T(8,128)(2,1)}, bf16[513,384]{1,0:T(8,128)(2,1)}, u32[]{:S(2)}, u32[]{:S(2)}) collective-permute-start(bf16[513,384]{1,0:T(8,128)(2,1)} %copy.78), channel_id=1, source_target_pairs={{0,8},{8,16},{16,24},{24,32},{32,40},{40,48},{48,56},{56,64},{64,7... | collective-permute-start | bytes 1181960 | tf_op jit(solution)/shard_map/while/body/eval_jaxpr/ppermute | solution.py:18
  198.3 10.7 %collective-permute-start = (bf16[513,384]{1,0:T(8,128)(2,1)}, bf16[513,384]{1,0:T(8,128)(2,1)}, u32[]{:S(2)}, u32[]{:S(2)}) collective-permute-start(bf16[513,384]{1,0:T(8,128)(2,1)} %copy.78), channel_id=1, source_target_pairs={{0,8},{8,16},{16,24},{24,32},{32,40},{40,48},{48,56},{56,64},{64,7... | collective-permute-start | bytes 1181960 | tf_op jit(solution)/shard_map/while/body/eval_jaxpr/ppermute | solution.py:18
  210.7 10.9 %collective-permute-start = (bf16[513,384]{1,0:T(8,128)(2,1)}, bf16[513,384]{1,0:T(8,128)(2,1)}, u32[]{:S(2)}, u32[]{:S(2)}) collective-permute-start(bf16[513,384]{1,0:T(8,128)(2,1)} %copy.78), channel_id=1, source_target_pairs={{0,8},{8,16},{16,24},{24,32},{32,40},{40,48},{48,56},{56,64},{64,7... | collective-permute-start | bytes 1181960 | tf_op jit(solution)/shard_map/while/body/eval_jaxpr/ppermute | solution.py:18
  223.4 16.5 %collective-permute-start = (bf16[513,384]{1,0:T(8,128)(2,1)}, bf16[513,384]{1,0:T(8,128)(2,1)}, u32[]{:S(2)}, u32[]{:S(2)}) collective-permute-start(bf16[513,384]{1,0:T(8,128)(2,1)} %copy.78), channel_id=1, source_target_pairs={{0,8},{8,16},{16,24},{24,32},{32,40},{40,48},{48,56},{56,64},{64,7... | collective-permute-start | bytes 1181960 | tf_op jit(solution)/shard_map/while/body/eval_jaxpr/ppermute | solution.py:18
  241.7 16.3 %collective-permute-start = (bf16[513,384]{1,0:T(8,128)(2,1)}, bf16[513,384]{1,0:T(8,128)(2,1)}, u32[]{:S(2)}, u32[]{:S(2)}) collective-permute-start(bf16[513,384]{1,0:T(8,128)(2,1)} %copy.78), channel_id=1, source_target_pairs={{0,8},{8,16},{16,24},{24,32},{32,40},{40,48},{48,56},{56,64},{64,7... | collective-permute-start | bytes 1181960 | tf_op jit(solution)/shard_map/while/body/eval_jaxpr/ppermute | solution.py:18
  259.8 16.8 %collective-permute-start = (bf16[513,384]{1,0:T(8,128)(2,1)}, bf16[513,384]{1,0:T(8,128)(2,1)}, u32[]{:S(2)}, u32[]{:S(2)}) collective-permute-start(bf16[513,384]{1,0:T(8,128)(2,1)} %copy.78), channel_id=1, source_target_pairs={{0,8},{8,16},{16,24},{24,32},{32,40},{40,48},{48,56},{56,64},{64,7... | collective-permute-start | bytes 1181960 | tf_op jit(solution)/shard_map/while/body/eval_jaxpr/ppermute | solution.py:18
  278.3 16.6 %collective-permute-start = (bf16[513,384]{1,0:T(8,128)(2,1)}, bf16[513,384]{1,0:T(8,128)(2,1)}, u32[]{:S(2)}, u32[]{:S(2)}) collective-permute-start(bf16[513,384]{1,0:T(8,128)(2,1)} %copy.78), channel_id=1, source_target_pairs={{0,8},{8,16},{16,24},{24,32},{32,40},{40,48},{48,56},{56,64},{64,7... | collective-permute-start | bytes 1181960 | tf_op jit(solution)/shard_map/while/body/eval_jaxpr/ppermute | solution.py:18
  296.6 15.8 %collective-permute-start = (bf16[513,384]{1,0:T(8,128)(2,1)}, bf16[513,384]{1,0:T(8,128)(2,1)}, u32[]{:S(2)}, u32[]{:S(2)}) collective-permute-start(bf16[513,384]{1,0:T(8,128)(2,1)} %copy.78), channel_id=1, source_target_pairs={{0,8},{8,16},{16,24},{24,32},{32,40},{40,48},{48,56},{56,64},{64,7... | collective-permute-start | bytes 1181960 | tf_op jit(solution)/shard_map/while/body/eval_jaxpr/ppermute | solution.py:18
  314.2 14.5 %collective-permute-start = (bf16[513,384]{1,0:T(8,128)(2,1)}, bf16[513,384]{1,0:T(8,128)(2,1)}, u32[]{:S(2)}, u32[]{:S(2)}) collective-permute-start(bf16[513,384]{1,0:T(8,128)(2,1)} %copy.78), channel_id=1, source_target_pairs={{0,8},{8,16},{16,24},{24,32},{32,40},{40,48},{48,56},{56,64},{64,7... | collective-permute-start | bytes 1181960 | tf_op jit(solution)/shard_map/while/body/eval_jaxpr/ppermute | solution.py:18
  330.4 12.5 %collective-permute-start = (bf16[513,384]{1,0:T(8,128)(2,1)}, bf16[513,384]{1,0:T(8,128)(2,1)}, u32[]{:S(2)}, u32[]{:S(2)}) collective-permute-start(bf16[513,384]{1,0:T(8,128)(2,1)} %copy.78), channel_id=1, source_target_pairs={{0,8},{8,16},{16,24},{24,32},{32,40},{40,48},{48,56},{56,64},{64,7... | collective-permute-start | bytes 1181960 | tf_op jit(solution)/shard_map/while/body/eval_jaxpr/ppermute | solution.py:18
  344.7 12.5 %collective-permute-start = (bf16[513,384]{1,0:T(8,128)(2,1)}, bf16[513,384]{1,0:T(8,128)(2,1)}, u32[]{:S(2)}, u32[]{:S(2)}) collective-permute-start(bf16[513,384]{1,0:T(8,128)(2,1)} %copy.78), channel_id=1, source_target_pairs={{0,8},{8,16},{16,24},{24,32},{32,40},{40,48},{48,56},{56,64},{64,7... | collective-permute-start | bytes 1181960 | tf_op jit(solution)/shard_map/while/body/eval_jaxpr/ppermute | solution.py:18
  358.9 12.5 %collective-permute-start = (bf16[513,384]{1,0:T(8,128)(2,1)}, bf16[513,384]{1,0:T(8,128)(2,1)}, u32[]{:S(2)}, u32[]{:S(2)}) collective-permute-start(bf16[513,384]{1,0:T(8,128)(2,1)} %copy.78), channel_id=1, source_target_pairs={{0,8},{8,16},{16,24},{24,32},{32,40},{40,48},{48,56},{56,64},{64,7... | collective-permute-start | bytes 1181960 | tf_op jit(solution)/shard_map/while/body/eval_jaxpr/ppermute | solution.py:18
  373.2 13.1 %collective-permute-start = (bf16[513,384]{1,0:T(8,128)(2,1)}, bf16[513,384]{1,0:T(8,128)(2,1)}, u32[]{:S(2)}, u32[]{:S(2)}) collective-permute-start(bf16[513,384]{1,0:T(8,128)(2,1)} %copy.78), channel_id=1, source_target_pairs={{0,8},{8,16},{16,24},{24,32},{32,40},{40,48},{48,56},{56,64},{64,7... | collective-permute-start | bytes 1181960 | tf_op jit(solution)/shard_map/while/body/eval_jaxpr/ppermute | solution.py:18
  388.1 13.8 %collective-permute-start = (bf16[513,384]{1,0:T(8,128)(2,1)}, bf16[513,384]{1,0:T(8,128)(2,1)}, u32[]{:S(2)}, u32[]{:S(2)}) collective-permute-start(bf16[513,384]{1,0:T(8,128)(2,1)} %copy.78), channel_id=1, source_target_pairs={{0,8},{8,16},{16,24},{24,32},{32,40},{40,48},{48,56},{56,64},{64,7... | collective-permute-start | bytes 1181960 | tf_op jit(solution)/shard_map/while/body/eval_jaxpr/ppermute | solution.py:18
  403.6 13.8 %collective-permute-start = (bf16[513,384]{1,0:T(8,128)(2,1)}, bf16[513,384]{1,0:T(8,128)(2,1)}, u32[]{:S(2)}, u32[]{:S(2)}) collective-permute-start(bf16[513,384]{1,0:T(8,128)(2,1)} %copy.78), channel_id=1, source_target_pairs={{0,8},{8,16},{16,24},{24,32},{32,40},{40,48},{48,56},{56,64},{64,7... | collective-permute-start | bytes 1181960 | tf_op jit(solution)/shard_map/while/body/eval_jaxpr/ppermute | solution.py:18
  419.3 13.7 %collective-permute-start = (bf16[513,384]{1,0:T(8,128)(2,1)}, bf16[513,384]{1,0:T(8,128)(2,1)}, u32[]{:S(2)}, u32[]{:S(2)}) collective-permute-start(bf16[513,384]{1,0:T(8,128)(2,1)} %copy.78), channel_id=1, source_target_pairs={{0,8},{8,16},{16,24},{24,32},{32,40},{40,48},{48,56},{56,64},{64,7... | collective-permute-start | bytes 1181960 | tf_op jit(solution)/shard_map/while/body/eval_jaxpr/ppermute | solution.py:18
  434.7 13.6 %collective-permute-start = (bf16[513,384]{1,0:T(8,128)(2,1)}, bf16[513,384]{1,0:T(8,128)(2,1)}, u32[]{:S(2)}, u32[]{:S(2)}) collective-permute-start(bf16[513,384]{1,0:T(8,128)(2,1)} %copy.78), channel_id=1, source_target_pairs={{0,8},{8,16},{16,24},{24,32},{32,40},{40,48},{48,56},{56,64},{64,7... | collective-permute-start | bytes 1181960 | tf_op jit(solution)/shard_map/while/body/eval_jaxpr/ppermute | solution.py:18
  450.2 13.6 %collective-permute-start = (bf16[513,384]{1,0:T(8,128)(2,1)}, bf16[513,384]{1,0:T(8,128)(2,1)}, u32[]{:S(2)}, u32[]{:S(2)}) collective-permute-start(bf16[513,384]{1,0:T(8,128)(2,1)} %copy.78), channel_id=1, source_target_pairs={{0,8},{8,16},{16,24},{24,32},{32,40},{40,48},{48,56},{56,64},{64,7... | collective-permute-start | bytes 1181960 | tf_op jit(solution)/shard_map/while/body/eval_jaxpr/ppermute | solution.py:18
  465.5 13.6 %collective-permute-start = (bf16[513,384]{1,0:T(8,128)(2,1)}, bf16[513,384]{1,0:T(8,128)(2,1)}, u32[]{:S(2)}, u32[]{:S(2)}) collective-permute-start(bf16[513,384]{1,0:T(8,128)(2,1)} %copy.78), channel_id=1, source_target_pairs={{0,8},{8,16},{16,24},{24,32},{32,40},{40,48},{48,56},{56,64},{64,7... | collective-permute-start | bytes 1181960 | tf_op jit(solution)/shard_map/while/body/eval_jaxpr/ppermute | solution.py:18
  480.8 13.5 %collective-permute-start = (bf16[513,384]{1,0:T(8,128)(2,1)}, bf16[513,384]{1,0:T(8,128)(2,1)}, u32[]{:S(2)}, u32[]{:S(2)}) collective-permute-start(bf16[513,384]{1,0:T(8,128)(2,1)} %copy.78), channel_id=1, source_target_pairs={{0,8},{8,16},{16,24},{24,32},{32,40},{40,48},{48,56},{56,64},{64,7... | collective-permute-start | bytes 1181960 | tf_op jit(solution)/shard_map/while/body/eval_jaxpr/ppermute | solution.py:18
  (24 other events, 978.3 us)
Sparse Core Ops, SparseCore 0:
  503.5 148.0 reduce-scatter.3
where the time goes:
time: 684 us; the launch traced here: 679 us
  local copies, waits for them, and re-layouts  171 us (25%)
  starting transfers between devices  162 us (24%)
  waiting for transfers between devices  147 us (21%)
  matrix products  118 us (17%)
  blocking collectives  46.7 us (7%)
  other arithmetic  18.6 us (3%)
  between operations  14.4 us (2%)
    ppermute x32, starting transfers between devices, passed_along(): return lax.ppermute(block, axis, route)  162 us
    unnamed x2, waiting for transfers between devices  147 us
    dot_general x33, matrix products, attend(): jnp.einsum('hqk,khd->hqd', unnormed.astype(jnp.bfloat16), val_heads, pref...  69.6 us
    slice x64, local copies, waits for them, and re-layouts, attend(): val_heads = block[1].reshape(key_count, head_count, HEAD_DIM)  59.8 us
    another operation x31, local copies, waits for them, and re-layouts  55 us
    dot_general x33, matrix products, attend(): jnp.einsum('qhd,khd->hqk', query_heads, key_heads, preferred_element_type...  45.9 us
    pmin x1, blocking collectives, per_device(): first_tok = lax.pmin(local_first, 'seq')  28.3 us
    slice x32, local copies, waits for them, and re-layouts, attend(): key_heads = block[0].reshape(key_count, head_count, HEAD_DIM)  25.6 us
  transfers between devices with their start and end apart: 33, of which 2 were waited for; matrix products, arithmetic and copies ran while one was open for 35% of the time, Pallas kernels for 0%

commit v1 on v0

--- a/solution.py
+++ b/solution.py
@@ -3,6 +3,7 @@
 import jax.numpy as jnp
 from jax import lax
 from jax.sharding import PartitionSpec as P
+from jax.lax import all_gather
 
 D = 3072
 HEAD_DIM = 96
@@ -10,6 +11,10 @@
 far_index = 1073741824
 masked_score = -1e30
 norm_epsilon = 1e-05
+
+
+def _choose_edge(in_array):
+    return all_gather(in_array, axis_name="tp").sum(axis=0)
 
 
 def passed_along(block, axis, distance):
@@ -133,7 +138,7 @@
     ).astype(jnp.float32)
     hidden_out = (hidden.astype(jnp.float32) + own_sum).astype(jnp.bfloat16)
     stream_wide = hidden_out.astype(jnp.float32)
-    square_total = lax.psum(jnp.sum(stream_wide * stream_wide, axis=1), "tp")
+    square_total = _choose_edge(jnp.sum(stream_wide * stream_wide, axis=1))
     normed = (
         stream_wide
         * lax.rsqrt(square_total / D + norm_epsilon)[:, None]

time: 684 us -> 684 us (level)
    psum x1 -> x0, blocking collectives: 18.4 us -> none  [per_device(): square_total = lax.psum(jnp.sum(stream_wide * stream_wide, axis=1), 'tp')]
    all_gather x0 -> x1, blocking collectives: none -> 17.5 us  [_choose_edge(): return all_gather(in_array, axis_name='tp').sum(axis=0)]
where the time goes in v1:
time: 684 us; the launch traced here: 678 us
  local copies, waits for them, and re-layouts  171 us (25%)
  starting transfers between devices  162 us (24%)
  waiting for transfers between devices  147 us (21%)
  matrix products  118 us (17%)
  blocking collectives  45.8 us (7%)
  other arithmetic  18.6 us (3%)
  between operations  14.4 us (2%)
    ppermute x32, starting transfers between devices, passed_along(): return lax.ppermute(block, axis, route)  162 us
    unnamed x2, waiting for transfers between devices  147 us
    dot_general x33, matrix products, attend(): jnp.einsum('hqk,khd->hqd', unnormed.astype(jnp.bfloat16), val_heads, pref...  69.6 us
    slice x64, local copies, waits for them, and re-layouts, attend(): val_heads = block[1].reshape(key_count, head_count, HEAD_DIM)  59.8 us
    another operation x31, local copies, waits for them, and re-layouts  55 us
    dot_general x33, matrix products, attend(): jnp.einsum('qhd,khd->hqk', query_heads, key_heads, preferred_element_type...  45.9 us
    pmin x1, blocking collectives, per_device(): first_tok = lax.pmin(local_first, 'seq')  28.3 us
    slice x32, local copies, waits for them, and re-layouts, attend(): key_heads = block[0].reshape(key_count, head_count, HEAD_DIM)  25.6 us
  transfers between devices with their start and end apart: 33, of which 2 were waited for; matrix products, arithmetic and copies ran while one was open for 35% of the time, Pallas kernels for 0%

profile of v1, /device:TPU:8, one launch (start us, length us, event | category | flops | bytes accessed | tf_op | source)
XLA Modules:
  0.0 678.0 jit_solution(3858717579963422848)
XLA Ops:
  8.2 28.3 %pmin.7 = s32[32]{0:T(128)S(1)} all-reduce(s32[32]{0:T(128)S(1)} %select_reduce_fusion.1), channel_id=1, replica_groups=mesh['seq'=64,'tp'=8] {'seq'}, use_global_device_ids=true, to_apply=%region_1.2 | all-reduce | flops 32 | bytes 256 | tf_op jit(solution)/shard_map/pmin | solution.py:90
  50.9 443.5 %while.16 = (s32[]{:T(128)}, f32[4,256]{1,0:T(4,128)S(1)}, f32[4,256]{1,0:T(4,128)S(1)}, f32[4,256,96]{1,2,0:T(8,128)}, bf16[513,384]{1,0:T(8,128)(2,1)}, /*inde...) while((s32[]{:T(128)}, f32[4,256]{1,0:T(4,128)S(1)}, f32[4,256]{1,0:T(4,128)S(1)}, ...), condition=%wide.region_8.9_spmd, body=%wide.region_5.8_spmd.sunk | while | flops 103286784 | bytes 8788605 | solution.py:126
  111.1 3.4 collective-permute-start
  160.9 3.3 collective-permute-start
  210.7 3.5 collective-permute-start
  223.4 9.2 %collective-permute-start = (bf16[513,384]{1,0:T(8,128)(2,1)}, bf16[513,384]{1,0:T(8,128)(2,1)}, u32[]{:S(2)}, u32[]{:S(2)}) collective-permute-start(bf16[513,384]{1,0:T(8,128)(2,1)} %copy.78), channel_id=1, source_target_pairs={{0,8},{8,16},{16,24},{24,32},{32,40},{40,48},{48,56},{56,64},{64,7... | collective-permute-start | bytes 1181960 | tf_op jit(solution)/shard_map/while/body/eval_jaxpr/ppermute | solution.py:23
  241.7 8.9 %collective-permute-start = (bf16[513,384]{1,0:T(8,128)(2,1)}, bf16[513,384]{1,0:T(8,128)(2,1)}, u32[]{:S(2)}, u32[]{:S(2)}) collective-permute-start(bf16[513,384]{1,0:T(8,128)(2,1)} %copy.78), channel_id=1, source_target_pairs={{0,8},{8,16},{16,24},{24,32},{32,40},{40,48},{48,56},{56,64},{64,7... | collective-permute-start | bytes 1181960 | tf_op jit(solution)/shard_map/while/body/eval_jaxpr/ppermute | solution.py:23
  259.8 9.4 %collective-permute-start = (bf16[513,384]{1,0:T(8,128)(2,1)}, bf16[513,384]{1,0:T(8,128)(2,1)}, u32[]{:S(2)}, u32[]{:S(2)}) collective-permute-start(bf16[513,384]{1,0:T(8,128)(2,1)} %copy.78), channel_id=1, source_target_pairs={{0,8},{8,16},{16,24},{24,32},{32,40},{40,48},{48,56},{56,64},{64,7... | collective-permute-start | bytes 1181960 | tf_op jit(solution)/shard_map/while/body/eval_jaxpr/ppermute | solution.py:23
  278.3 9.2 %collective-permute-start = (bf16[513,384]{1,0:T(8,128)(2,1)}, bf16[513,384]{1,0:T(8,128)(2,1)}, u32[]{:S(2)}, u32[]{:S(2)}) collective-permute-start(bf16[513,384]{1,0:T(8,128)(2,1)} %copy.78), channel_id=1, source_target_pairs={{0,8},{8,16},{16,24},{24,32},{32,40},{40,48},{48,56},{56,64},{64,7... | collective-permute-start | bytes 1181960 | tf_op jit(solution)/shard_map/while/body/eval_jaxpr/ppermute | solution.py:23
  296.6 8.4 %collective-permute-start = (bf16[513,384]{1,0:T(8,128)(2,1)}, bf16[513,384]{1,0:T(8,128)(2,1)}, u32[]{:S(2)}, u32[]{:S(2)}) collective-permute-start(bf16[513,384]{1,0:T(8,128)(2,1)} %copy.78), channel_id=1, source_target_pairs={{0,8},{8,16},{16,24},{24,32},{32,40},{40,48},{48,56},{56,64},{64,7... | collective-permute-start | bytes 1181960 | tf_op jit(solution)/shard_map/while/body/eval_jaxpr/ppermute | solution.py:23
  314.2 7.1 %collective-permute-start = (bf16[513,384]{1,0:T(8,128)(2,1)}, bf16[513,384]{1,0:T(8,128)(2,1)}, u32[]{:S(2)}, u32[]{:S(2)}) collective-permute-start(bf16[513,384]{1,0:T(8,128)(2,1)} %copy.78), channel_id=1, source_target_pairs={{0,8},{8,16},{16,24},{24,32},{32,40},{40,48},{48,56},{56,64},{64,7... | collective-permute-start | bytes 1181960 | tf_op jit(solution)/shard_map/while/body/eval_jaxpr/ppermute | solution.py:23
  330.4 5.1 collective-permute-start
  344.7 5.1 collective-permute-start
  358.9 5.1 collective-permute-start
  373.2 5.7 collective-permute-start
  388.1 6.5 collective-permute-start
  403.6 6.5 collective-permute-start
  419.3 6.4 collective-permute-start
  434.7 6.3 collective-permute-start
  450.2 6.2 collective-permute-start
  465.5 6.2 collective-permute-start
  480.8 6.2 collective-permute-start
  504.7 146.8 %reduce-scatter.4.cloned.1.call-done = bf16[384,256]{1,0:T(8,128)(2,1)} async-done(((bf16[3072,256]{1,0:T(8,128)(2,1)}), bf16[384,256]{1,0:T(8,128)(2,1)}) %reduce-scatter.4.cloned.1.call-update) | async-done | bytes 196624
  652.8 17.5 %all-gather.1 = f32[8,1,256]{2,1,0:T(1,128)S(1)} all-gather(f32[1,1,256]{2,1,0:T(1,128)S(1)} %bitcast.53), channel_id=2, replica_groups=mesh['seq'=64,'tp'=8] {'tp'}, dimensions={0}, use_global_device_ids=true | all-gather | bytes 9216 | tf_op jit(solution)/shard_map/all_gather | solution.py:17
  (498 shorter events, 342.0 us)
Async XLA Ops:
  7.2 644.4 %reduce-scatter.4.cloned.1.call-start = ((), (), s32[]{:S(2)}) async-start(), calls=%async_computation.1 | async-start | bytes 1769472
  111.1 10.7 %collective-permute-start = (bf16[513,384]{1,0:T(8,128)(2,1)}, bf16[513,384]{1,0:T(8,128)(2,1)}, u32[]{:S(2)}, u32[]{:S(2)}) collective-permute-start(bf16[513,384]{1,0:T(8,128)(2,1)} %copy.78), channel_id=1, source_target_pairs={{0,8},{8,16},{16,24},{24,32},{32,40},{40,48},{48,56},{56,64},{64,7... | collective-permute-start | bytes 1181960 | tf_op jit(solution)/shard_map/while/body/eval_jaxpr/ppermute | solution.py:23
  123.6 10.7 %collective-permute-start = (bf16[513,384]{1,0:T(8,128)(2,1)}, bf16[513,384]{1,0:T(8,128)(2,1)}, u32[]{:S(2)}, u32[]{:S(2)}) collective-permute-start(bf16[513,384]{1,0:T(8,128)(2,1)} %copy.78), channel_id=1, source_target_pairs={{0,8},{8,16},{16,24},{24,32},{32,40},{40,48},{48,56},{56,64},{64,7... | collective-permute-start | bytes 1181960 | tf_op jit(solution)/shard_map/while/body/eval_jaxpr/ppermute | solution.py:23
  160.9 10.7 %collective-permute-start = (bf16[513,384]{1,0:T(8,128)(2,1)}, bf16[513,384]{1,0:T(8,128)(2,1)}, u32[]{:S(2)}, u32[]{:S(2)}) collective-permute-start(bf16[513,384]{1,0:T(8,128)(2,1)} %copy.78), channel_id=1, source_target_pairs={{0,8},{8,16},{16,24},{24,32},{32,40},{40,48},{48,56},{56,64},{64,7... | collective-permute-start | bytes 1181960 | tf_op jit(solution)/shard_map/while/body/eval_jaxpr/ppermute | solution.py:23
  173.4 10.7 %collective-permute-start = (bf16[513,384]{1,0:T(8,128)(2,1)}, bf16[513,384]{1,0:T(8,128)(2,1)}, u32[]{:S(2)}, u32[]{:S(2)}) collective-permute-start(bf16[513,384]{1,0:T(8,128)(2,1)} %copy.78), channel_id=1, source_target_pairs={{0,8},{8,16},{16,24},{24,32},{32,40},{40,48},{48,56},{56,64},{64,7... | collective-permute-start | bytes 1181960 | tf_op jit(solution)/shard_map/while/body/eval_jaxpr/ppermute | solution.py:23
  198.3 10.7 %collective-permute-start = (bf16[513,384]{1,0:T(8,128)(2,1)}, bf16[513,384]{1,0:T(8,128)(2,1)}, u32[]{:S(2)}, u32[]{:S(2)}) collective-permute-start(bf16[513,384]{1,0:T(8,128)(2,1)} %copy.78), channel_id=1, source_target_pairs={{0,8},{8,16},{16,24},{24,32},{32,40},{40,48},{48,56},{56,64},{64,7... | collective-permute-start | bytes 1181960 | tf_op jit(solution)/shard_map/while/body/eval_jaxpr/ppermute | solution.py:23
  210.7 10.9 %collective-permute-start = (bf16[513,384]{1,0:T(8,128)(2,1)}, bf16[513,384]{1,0:T(8,128)(2,1)}, u32[]{:S(2)}, u32[]{:S(2)}) collective-permute-start(bf16[513,384]{1,0:T(8,128)(2,1)} %copy.78), channel_id=1, source_target_pairs={{0,8},{8,16},{16,24},{24,32},{32,40},{40,48},{48,56},{56,64},{64,7... | collective-permute-start | bytes 1181960 | tf_op jit(solution)/shard_map/while/body/eval_jaxpr/ppermute | solution.py:23
  223.4 16.5 %collective-permute-start = (bf16[513,384]{1,0:T(8,128)(2,1)}, bf16[513,384]{1,0:T(8,128)(2,1)}, u32[]{:S(2)}, u32[]{:S(2)}) collective-permute-start(bf16[513,384]{1,0:T(8,128)(2,1)} %copy.78), channel_id=1, source_target_pairs={{0,8},{8,16},{16,24},{24,32},{32,40},{40,48},{48,56},{56,64},{64,7... | collective-permute-start | bytes 1181960 | tf_op jit(solution)/shard_map/while/body/eval_jaxpr/ppermute | solution.py:23
  241.7 16.3 %collective-permute-start = (bf16[513,384]{1,0:T(8,128)(2,1)}, bf16[513,384]{1,0:T(8,128)(2,1)}, u32[]{:S(2)}, u32[]{:S(2)}) collective-permute-start(bf16[513,384]{1,0:T(8,128)(2,1)} %copy.78), channel_id=1, source_target_pairs={{0,8},{8,16},{16,24},{24,32},{32,40},{40,48},{48,56},{56,64},{64,7... | collective-permute-start | bytes 1181960 | tf_op jit(solution)/shard_map/while/body/eval_jaxpr/ppermute | solution.py:23
  259.8 16.8 %collective-permute-start = (bf16[513,384]{1,0:T(8,128)(2,1)}, bf16[513,384]{1,0:T(8,128)(2,1)}, u32[]{:S(2)}, u32[]{:S(2)}) collective-permute-start(bf16[513,384]{1,0:T(8,128)(2,1)} %copy.78), channel_id=1, source_target_pairs={{0,8},{8,16},{16,24},{24,32},{32,40},{40,48},{48,56},{56,64},{64,7... | collective-permute-start | bytes 1181960 | tf_op jit(solution)/shard_map/while/body/eval_jaxpr/ppermute | solution.py:23
  278.3 16.6 %collective-permute-start = (bf16[513,384]{1,0:T(8,128)(2,1)}, bf16[513,384]{1,0:T(8,128)(2,1)}, u32[]{:S(2)}, u32[]{:S(2)}) collective-permute-start(bf16[513,384]{1,0:T(8,128)(2,1)} %copy.78), channel_id=1, source_target_pairs={{0,8},{8,16},{16,24},{24,32},{32,40},{40,48},{48,56},{56,64},{64,7... | collective-permute-start | bytes 1181960 | tf_op jit(solution)/shard_map/while/body/eval_jaxpr/ppermute | solution.py:23
  296.6 15.8 %collective-permute-start = (bf16[513,384]{1,0:T(8,128)(2,1)}, bf16[513,384]{1,0:T(8,128)(2,1)}, u32[]{:S(2)}, u32[]{:S(2)}) collective-permute-start(bf16[513,384]{1,0:T(8,128)(2,1)} %copy.78), channel_id=1, source_target_pairs={{0,8},{8,16},{16,24},{24,32},{32,40},{40,48},{48,56},{56,64},{64,7... | collective-permute-start | bytes 1181960 | tf_op jit(solution)/shard_map/while/body/eval_jaxpr/ppermute | solution.py:23
  314.2 14.5 %collective-permute-start = (bf16[513,384]{1,0:T(8,128)(2,1)}, bf16[513,384]{1,0:T(8,128)(2,1)}, u32[]{:S(2)}, u32[]{:S(2)}) collective-permute-start(bf16[513,384]{1,0:T(8,128)(2,1)} %copy.78), channel_id=1, source_target_pairs={{0,8},{8,16},{16,24},{24,32},{32,40},{40,48},{48,56},{56,64},{64,7... | collective-permute-start | bytes 1181960 | tf_op jit(solution)/shard_map/while/body/eval_jaxpr/ppermute | solution.py:23
  330.4 12.5 %collective-permute-start = (bf16[513,384]{1,0:T(8,128)(2,1)}, bf16[513,384]{1,0:T(8,128)(2,1)}, u32[]{:S(2)}, u32[]{:S(2)}) collective-permute-start(bf16[513,384]{1,0:T(8,128)(2,1)} %copy.78), channel_id=1, source_target_pairs={{0,8},{8,16},{16,24},{24,32},{32,40},{40,48},{48,56},{56,64},{64,7... | collective-permute-start | bytes 1181960 | tf_op jit(solution)/shard_map/while/body/eval_jaxpr/ppermute | solution.py:23
  344.7 12.5 %collective-permute-start = (bf16[513,384]{1,0:T(8,128)(2,1)}, bf16[513,384]{1,0:T(8,128)(2,1)}, u32[]{:S(2)}, u32[]{:S(2)}) collective-permute-start(bf16[513,384]{1,0:T(8,128)(2,1)} %copy.78), channel_id=1, source_target_pairs={{0,8},{8,16},{16,24},{24,32},{32,40},{40,48},{48,56},{56,64},{64,7... | collective-permute-start | bytes 1181960 | tf_op jit(solution)/shard_map/while/body/eval_jaxpr/ppermute | solution.py:23
  358.9 12.5 %collective-permute-start = (bf16[513,384]{1,0:T(8,128)(2,1)}, bf16[513,384]{1,0:T(8,128)(2,1)}, u32[]{:S(2)}, u32[]{:S(2)}) collective-permute-start(bf16[513,384]{1,0:T(8,128)(2,1)} %copy.78), channel_id=1, source_target_pairs={{0,8},{8,16},{16,24},{24,32},{32,40},{40,48},{48,56},{56,64},{64,7... | collective-permute-start | bytes 1181960 | tf_op jit(solution)/shard_map/while/body/eval_jaxpr/ppermute | solution.py:23
  373.2 13.1 %collective-permute-start = (bf16[513,384]{1,0:T(8,128)(2,1)}, bf16[513,384]{1,0:T(8,128)(2,1)}, u32[]{:S(2)}, u32[]{:S(2)}) collective-permute-start(bf16[513,384]{1,0:T(8,128)(2,1)} %copy.78), channel_id=1, source_target_pairs={{0,8},{8,16},{16,24},{24,32},{32,40},{40,48},{48,56},{56,64},{64,7... | collective-permute-start | bytes 1181960 | tf_op jit(solution)/shard_map/while/body/eval_jaxpr/ppermute | solution.py:23
  388.1 13.8 %collective-permute-start = (bf16[513,384]{1,0:T(8,128)(2,1)}, bf16[513,384]{1,0:T(8,128)(2,1)}, u32[]{:S(2)}, u32[]{:S(2)}) collective-permute-start(bf16[513,384]{1,0:T(8,128)(2,1)} %copy.78), channel_id=1, source_target_pairs={{0,8},{8,16},{16,24},{24,32},{32,40},{40,48},{48,56},{56,64},{64,7... | collective-permute-start | bytes 1181960 | tf_op jit(solution)/shard_map/while/body/eval_jaxpr/ppermute | solution.py:23
  403.6 13.8 %collective-permute-start = (bf16[513,384]{1,0:T(8,128)(2,1)}, bf16[513,384]{1,0:T(8,128)(2,1)}, u32[]{:S(2)}, u32[]{:S(2)}) collective-permute-start(bf16[513,384]{1,0:T(8,128)(2,1)} %copy.78), channel_id=1, source_target_pairs={{0,8},{8,16},{16,24},{24,32},{32,40},{40,48},{48,56},{56,64},{64,7... | collective-permute-start | bytes 1181960 | tf_op jit(solution)/shard_map/while/body/eval_jaxpr/ppermute | solution.py:23
  419.3 13.7 %collective-permute-start = (bf16[513,384]{1,0:T(8,128)(2,1)}, bf16[513,384]{1,0:T(8,128)(2,1)}, u32[]{:S(2)}, u32[]{:S(2)}) collective-permute-start(bf16[513,384]{1,0:T(8,128)(2,1)} %copy.78), channel_id=1, source_target_pairs={{0,8},{8,16},{16,24},{24,32},{32,40},{40,48},{48,56},{56,64},{64,7... | collective-permute-start | bytes 1181960 | tf_op jit(solution)/shard_map/while/body/eval_jaxpr/ppermute | solution.py:23
  434.7 13.6 %collective-permute-start = (bf16[513,384]{1,0:T(8,128)(2,1)}, bf16[513,384]{1,0:T(8,128)(2,1)}, u32[]{:S(2)}, u32[]{:S(2)}) collective-permute-start(bf16[513,384]{1,0:T(8,128)(2,1)} %copy.78), channel_id=1, source_target_pairs={{0,8},{8,16},{16,24},{24,32},{32,40},{40,48},{48,56},{56,64},{64,7... | collective-permute-start | bytes 1181960 | tf_op jit(solution)/shard_map/while/body/eval_jaxpr/ppermute | solution.py:23
  450.2 13.6 %collective-permute-start = (bf16[513,384]{1,0:T(8,128)(2,1)}, bf16[513,384]{1,0:T(8,128)(2,1)}, u32[]{:S(2)}, u32[]{:S(2)}) collective-permute-start(bf16[513,384]{1,0:T(8,128)(2,1)} %copy.78), channel_id=1, source_target_pairs={{0,8},{8,16},{16,24},{24,32},{32,40},{40,48},{48,56},{56,64},{64,7... | collective-permute-start | bytes 1181960 | tf_op jit(solution)/shard_map/while/body/eval_jaxpr/ppermute | solution.py:23
  465.5 13.6 %collective-permute-start = (bf16[513,384]{1,0:T(8,128)(2,1)}, bf16[513,384]{1,0:T(8,128)(2,1)}, u32[]{:S(2)}, u32[]{:S(2)}) collective-permute-start(bf16[513,384]{1,0:T(8,128)(2,1)} %copy.78), channel_id=1, source_target_pairs={{0,8},{8,16},{16,24},{24,32},{32,40},{40,48},{48,56},{56,64},{64,7... | collective-permute-start | bytes 1181960 | tf_op jit(solution)/shard_map/while/body/eval_jaxpr/ppermute | solution.py:23
  480.8 13.5 %collective-permute-start = (bf16[513,384]{1,0:T(8,128)(2,1)}, bf16[513,384]{1,0:T(8,128)(2,1)}, u32[]{:S(2)}, u32[]{:S(2)}) collective-permute-start(bf16[513,384]{1,0:T(8,128)(2,1)} %copy.78), channel_id=1, source_target_pairs={{0,8},{8,16},{16,24},{24,32},{32,40},{40,48},{48,56},{56,64},{64,7... | collective-permute-start | bytes 1181960 | tf_op jit(solution)/shard_map/while/body/eval_jaxpr/ppermute | solution.py:23
  (24 other events, 976.6 us)
Sparse Core Ops, SparseCore 0:
  503.5 148.0 reduce-scatter.3
